TPU v7x, 32 devices: a whole 2x2x4 slice. The times are simulated.
32 devices in a mesh: dp: 4 (over y, x), expert: 8 (over z, core).
Axes of the slice: x: 2, y: 2, z: 4, core: 2. Of those that a mesh axis runs over, the one named last changes fastest.
Arguments:
- tokens: bfloat16 [4096, 7168], P(('dp', 'expert')), may hold values from -6 to 6
- steering: float32 [7168], replicated, may hold values from -6 to 6
- norm_gain: float32 [7168], replicated, may hold values from 0.1 to 1.9
- route_ids: int32 [4096, 8], P(('dp', 'expert')), may hold values from 0 to 255, as said below
- route_gates: int32 [4096, 8], P(('dp', 'expert')), may hold values from 1 to 65535
- gate_weight: bfloat16 [7168, 8192], P(None, 'expert'), may hold values from -0.0625 to 0.0625
- up_weight: bfloat16 [7168, 8192], P(None, 'expert'), may hold values from -0.0625 to 0.0625
- down_weight: bfloat16 [8192, 7168], P('expert'), may hold values from -0.125 to 0.125
- out_grad: bfloat16 [4096, 7168], P(('dp', 'expert')), may hold values from -6 to 6
Outputs:
- layer_out: bfloat16 [4096, 7168], P(('dp', 'expert'))
- in_grad: bfloat16 [4096, 7168], P(('dp', 'expert'))
- steer_grad: float32 [7168], replicated
Inputs may be any that keep to these rules, and one draw needn't show every extreme that they name: `route_ids`: each row names 8 different experts. Among the 128 rows of one device no expert below 4 is named more than 8 times. One expert below 4, the same for every device, is named exactly 8 times by every device's rows, and on some devices every expert below 4 is named exactly 8 times.
All inputs are finite; a program needn't handle non-finite values.
Results may differ from a plain program's by a relative error of at most 0.0021.
Values may be sent and summed in bfloat16 or wider, within the bound.
No kernel may reach another device: no remote copies, remote signals or barrier semaphores. Data moves between devices by JAX's collectives and lax.ppermute only.
A program may use at most 128 MiB of HBM per device.

v0:
```python
import jax
import jax.numpy as jnp
from jax import lax
from jax.sharding import PartitionSpec as P

EXP_FLIGHT = 4
CAP = 8
EPSILON = 1e-06
GATE_UNIT = 1.0 / 65536.0


def slot_tables(route_ids, route_gates, flight, capacity):
    count_rows = route_ids.shape[0]
    expert_range = jnp.arange(flight, dtype=jnp.int32)
    hit_mask = route_ids[:, :, None] == expert_range[None, None, :]
    member = jnp.any(hit_mask, axis=1)
    scaled = route_gates.astype(jnp.float32) * GATE_UNIT
    weights = jnp.sum(jnp.where(hit_mask, scaled[:, :, None], 0.0), axis=1)
    position = jnp.cumsum(member.astype(jnp.int32), axis=0) - 1
    slot_of = jnp.where(member, position, capacity)
    slot_range = jnp.arange(capacity, dtype=jnp.int32)
    matches = slot_of[:, :, None] == slot_range[None, None, :]
    row_range = jnp.arange(count_rows, dtype=jnp.int32)
    slot_table = jnp.sum(jnp.where(matches, row_range[:, None, None], 0), axis=0)
    filled = jnp.any(matches, axis=0)
    combine = jnp.where(matches, weights[:, :, None], 0.0).reshape(count_rows, flight * capacity)
    return (slot_table, filled, combine)


def dispatch_rows(values, slot_table, filled):
    picked = values[slot_table]
    return jnp.where(filled[:, :, None], picked, jnp.zeros((), values.dtype))


def normalize(tokens, steering, norm_gain):
    residual = tokens.astype(jnp.float32) + steering
    inverse = lax.rsqrt(jnp.mean(residual * residual, axis=-1, keepdims=True) + EPSILON)
    normed = (residual * inverse * norm_gain).astype(jnp.bfloat16)
    return (residual, inverse, normed)


def norm_backward(residual, inverse, norm_gain, back_normed, out_grad):
    scaled = back_normed * norm_gain
    inner_mean = jnp.mean(scaled * residual, axis=-1, keepdims=True)
    cubed = inverse * inverse * inverse
    return out_grad.astype(jnp.float32) + inverse * scaled - residual * cubed * inner_mean


def share_forward(token_rows, gate_cols, up_cols, down_rows):
    gate_pre = jnp.dot(token_rows, gate_cols, preferred_element_type=jnp.float32)
    up_pre = jnp.dot(token_rows, up_cols, preferred_element_type=jnp.float32)
    hidden = (jax.nn.silu(gate_pre) * up_pre).astype(jnp.bfloat16)
    forward = jnp.dot(hidden, down_rows, preferred_element_type=jnp.float32).astype(jnp.bfloat16)
    return (forward, gate_pre, up_pre)


def share_backward(grad_rows, gate_pre, up_pre, gate_cols, up_cols, down_rows):
    contract = (((1,), (1,)), ((), ()))
    back_hidden = lax.dot_general(
        grad_rows, down_rows, contract, preferred_element_type=jnp.float32
    )
    sigmoid = jax.nn.sigmoid(gate_pre)
    back_up = (back_hidden * gate_pre * sigmoid).astype(jnp.bfloat16)
    back_gate = (back_hidden * up_pre * sigmoid * (1.0 + gate_pre * (1.0 - sigmoid))).astype(
        jnp.bfloat16
    )
    backward = lax.dot_general(back_gate, gate_cols, contract, preferred_element_type=jnp.float32)
    backward = backward + lax.dot_general(
        back_up, up_cols, contract, preferred_element_type=jnp.float32
    )
    return backward.astype(jnp.bfloat16)


def apply_combine(combine, partial_sums):
    return jnp.dot(combine, partial_sums, precision=lax.Precision.HIGHEST)


def shards(
    tokens,
    steering,
    norm_gain,
    route_ids,
    route_gates,
    gate_weight,
    up_weight,
    down_weight,
    out_grad,
):
    expert_count = lax.axis_size("expert")
    flight = EXP_FLIGHT
    group_size = expert_count // flight
    capacity = CAP
    feature_count = tokens.shape[1]
    residual, inverse, normed = normalize(tokens, steering, norm_gain)
    slot_table, filled, combine = slot_tables(route_ids, route_gates, flight, capacity)
    packed = jnp.stack(
        [dispatch_rows(normed, slot_table, filled), dispatch_rows(out_grad, slot_table, filled)],
        axis=1,
    )
    sending = jnp.repeat(packed, group_size, axis=0)
    arrived = lax.all_to_all(sending, "expert", split_axis=0, concat_axis=0, tiled=True)
    local_rows = arrived[:, 0].reshape(expert_count * capacity, feature_count)
    local_grads = arrived[:, 1].reshape(expert_count * capacity, feature_count)
    forward, gate_pre, up_pre = share_forward(local_rows, gate_weight, up_weight, down_weight)
    came_out = lax.all_to_all(
        forward.reshape(expert_count, capacity, feature_count),
        "expert",
        split_axis=0,
        concat_axis=0,
        tiled=True,
    )
    backward = share_backward(local_grads, gate_pre, up_pre, gate_weight, up_weight, down_weight)
    came_grad = lax.all_to_all(
        backward.reshape(expert_count, capacity, feature_count),
        "expert",
        split_axis=0,
        concat_axis=0,
        tiled=True,
    )
    out_sums = (
        came_out.reshape(flight, group_size, capacity, feature_count)
        .astype(jnp.float32)
        .sum(axis=1)
    )
    grad_sums = (
        came_grad.reshape(flight, group_size, capacity, feature_count)
        .astype(jnp.float32)
        .sum(axis=1)
    )
    mixture = apply_combine(combine, out_sums.reshape(flight * capacity, feature_count))
    back_normed = apply_combine(combine, grad_sums.reshape(flight * capacity, feature_count))
    layer_out = (residual + mixture).astype(jnp.bfloat16)
    total_grad = norm_backward(residual, inverse, norm_gain, back_normed, out_grad)
    steer_grad = lax.psum(jnp.sum(total_grad, axis=0), ("dp", "expert"))
    return (layer_out, total_grad.astype(jnp.bfloat16), steer_grad)


def solution(mesh):
    in_specs = (
        P(("dp", "expert"), None),
        P(),
        P(),
        P(("dp", "expert"), None),
        P(("dp", "expert"), None),
        P(None, "expert"),
        P(None, "expert"),
        P("expert", None),
        P(("dp", "expert"), None),
    )
    out_specs = (P(("dp", "expert"), None), P(("dp", "expert"), None), P())
    return jax.shard_map(shards, mesh=mesh, in_specs=in_specs, out_specs=out_specs, check_vma=False)
```

profile of v0, /device:TPU:0, one launch (start us, length us, event | category | flops | bytes accessed | tf_op | source)
XLA Modules:
  0.0 191.6 jit_solution(9282980750656883561)
XLA Ops:
  0.6 0.7 fusion.16
  1.3 0.1 copy.20
  1.5 0.2 reduce_window_sum.11
  1.6 0.1 copy.21
  1.7 0.2 select_reduce_fusion
  1.9 0.2 fusion.15
  2.0 0.1 reshape.94
  2.1 2.1 %multiply_reduce_fusion.1 = f32[128]{0:T(128)S(1)} fusion(bf16[128,7168]{1,0:T(8,128)(2,1)} %param.9, f32[7168]{0:T(1024)} %param.10), kind=kLoop, calls=%fused_computation.15 | loop fusion | flops 3669888 | bytes 1864192 | tf_op jit(solution)/shard_map/reduce_sum | solution.py:37
  4.2 2.1 %multiply_convert_fusion = bf16[128,7168]{1,0:T(8,128)(2,1)S(1)} fusion(bf16[128,7168]{1,0:T(8,128)(2,1)} %param.9, f32[7168]{0:T(1024)} %param.11, f32[128]{0:T(128)S(1)} %get-tuple-element.6, f32[7168]{0:T(1024)} %param.10), kind=kLoop, calls=%fused_computation.14 | loop fusion | flops 4587520 | bytes 3727872 | tf_op jit(solution)/shard_map/convert_element_type | solution.py:38
  6.3 0.8 gather_fusion
  7.1 3.0 %gather_fusion.1 = bf16[32,7168]{1,0:T(8,128)(2,1)S(1)} fusion(bf16[128,7168]{1,0:T(8,128)(2,1)} %param.17, s32[1024]{0:T(1024)S(1)} %pad_clamp_fusion), kind=kCustom, calls=%fused_computation.1 | custom fusion | bytes 917632 | tf_op jit(solution)/shard_map/gather | solution.py:31
  10.1 0.1 bitcast_select_fusion.1
  10.3 0.1 pad_maximum_fusion
  10.4 0.1 copy.22
  10.4 0.2 broadcast_in_dim.84
  10.6 49.6 %all_to_all.15 = bf16[8,2,8,7168]{3,2,1,0:T(8,128)(2,1)S(1)} all-to-all(bf16[8,2,8,7168]{3,2,1,0:T(8,128)(2,1)S(1)} %bitcast.44), channel_id=1, replica_groups=mesh['dp'=4,'expert'=8] {'expert'}, dimensions={0} | all-to-all | bytes 3670016 | tf_op jit(solution)/shard_map/all_to_all | solution.py:101
  60.2 7.9 %fusion.8 = f32[64,1024]{1,0:T(8,128)S(1)} fusion(bf16[7168,1024]{1,0:T(8,128)(2,1)} %param.14, bf16[8,2,8,7168]{3,2,1,0:T(8,128)(2,1)S(1)} %all_to_all.15), kind=kOutput, calls=%fused_computation.24 | convolution fusion | flops 939524096 | bytes 15859712 | tf_op jit(solution)/shard_map/dot_general | solution.py:50
  68.0 9.7 %fusion.6 = f32[64,1024]{1,0:T(8,128)S(1)} fusion(bf16[1024,7168]{1,0:T(8,128)(2,1)} %param.16, bf16[8,2,8,7168]{3,2,1,0:T(8,128)(2,1)S(1)} %all_to_all.15), kind=kOutput, calls=%fused_computation.20 | convolution fusion | flops 939524096 | bytes 15859712 | tf_op jit(solution)/shard_map/dot_general | solution.py:59
  77.8 7.9 %fusion.7 = f32[64,1024]{1,0:T(8,128)S(1)} fusion(bf16[7168,1024]{1,0:T(8,128)(2,1)} %param.15, bf16[8,2,8,7168]{3,2,1,0:T(8,128)(2,1)S(1)} %all_to_all.15), kind=kOutput, calls=%fused_computation.23 | convolution fusion | flops 939524096 | bytes 15859712 | tf_op jit(solution)/shard_map/dot_general | solution.py:51
  85.6 9.7 %fusion.9 = f32[64,7168]{1,0:T(8,128)S(1)} fusion(bf16[7168,1024]{1,0:T(8,128)(2,1)} %param.14, f32[64,1024]{1,0:T(8,128)S(1)} %fusion.8, f32[64,1024]{1,0:T(8,128)S(1)} %fusion.6, f32[64,1024]{1,0:T(8,128)S(1)} %fusion.7), kind=kOutput, calls=%fused_computation.31 | convolution fusion | flops 940179456 | bytes 17301504 | tf_op jit(solution)/shard_map/dot_general | solution.py:67
  95.4 10.9 %fusion.5 = bf16[8,8,7168]{2,1,0:T(8,128)(2,1)} fusion(f32[64,7168]{1,0:T(8,128)S(1)} %fusion.9, bf16[7168,1024]{1,0:T(8,128)(2,1)} %param.15, f32[64,1024]{1,0:T(8,128)S(1)} %fusion.6, f32[64,1024]{1,0:T(8,128)S(1)} %fusion.8), kind=kOutput, calls=%fused_computation.11 | convolution fusion | flops 940834816 | bytes 17956864 | tf_op jit(solution)/shard_map/dot_general | solution.py:68
  106.3 3.6 %all-to-all-start.2 = ((bf16[8,8,7168]{2,1,0:T(8,128)(2,1)}), bf16[8,8,7168]{2,1,0:T(8,128)(2,1)S(1)}, u32[]{:S(2)}, u32[]{:S(2)}) async-start(bf16[8,8,7168]{2,1,0:T(8,128)(2,1)} %fusion.5), calls=%async_computation.2 | async-start | bytes 1835008 | tf_op jit(solution)/shard_map/all_to_all | solution.py:113
  109.9 8.8 %fusion.4 = bf16[8,8,7168]{2,1,0:T(8,128)(2,1)} fusion(bf16[1024,7168]{1,0:T(8,128)(2,1)} %param.16, f32[64,1024]{1,0:T(8,128)S(1)} %fusion.7, f32[64,1024]{1,0:T(8,128)S(1)} %fusion.8), kind=kOutput, calls=%fused_computation.10 | convolution fusion | flops 940376064 | bytes 16121856 | tf_op jit(solution)/shard_map/dot_general | solution.py:53
  118.6 14.9 %all-to-all-done.2 = bf16[8,8,7168]{2,1,0:T(8,128)(2,1)S(1)} async-done(((bf16[8,8,7168]{2,1,0:T(8,128)(2,1)}), bf16[8,8,7168]{2,1,0:T(8,128)(2,1)S(1)}, u32[]{:S(2)}, u32[]{:S(2)}) %all-to-all-start.2) | async-done | bytes 917536 | tf_op jit(solution)/shard_map/all_to_all | solution.py:113
  133.5 0.9 copy-done.2
  134.4 3.6 %all-to-all-start.1 = ((bf16[8,8,7168]{2,1,0:T(8,128)(2,1)}), bf16[8,8,7168]{2,1,0:T(8,128)(2,1)S(1)}, u32[]{:S(2)}, u32[]{:S(2)}) async-start(bf16[8,8,7168]{2,1,0:T(8,128)(2,1)} %fusion.4), calls=%async_computation.1 | async-start | bytes 1835008 | tf_op jit(solution)/shard_map/all_to_all | solution.py:105
  138.1 1.4 convert_reduce_fusion
  139.5 3.6 %multiply_reduce_fusion = (f32[128]{0:T(128)S(1)}, f32[128,7168]{1,0:T(8,128)S(1)}) fusion(bf16[128,7168]{1,0:T(8,128)(2,1)S(1)} %copy-done, f32[7168]{0:T(1024)S(1)} %copy-done.3, f32[7168]{0:T(1024)S(1)} %copy-done.4, f32[4,8,7168]{2,1,0:T(8,128)S(1)} %convert_reduce_fusion, f32[128,4]{0,1:T(4,128)S(1)} %select_reduce_fusion.1, ...), kind=kOutput, calls=%fused_computation.13 | convolution fusion | flops 356917120 | bytes 6484480 | tf_op jit(solution)/shard_map/dot_general | solution.py:75
  143.2 2.6 %fusion.28 = (f32[7168]{0:T(1024)S(1)}, bf16[128,7168]{1,0:T(8,128)(2,1)}) fusion(f32[128]{0:T(128)S(1)} %broadcast_multiply_fusion, f32[128]{0:T(128)S(1)} %get-tuple-element.5, f32[7168]{0:T(1024)S(1)} %copy-done.3, bf16[128,7168]{1,0:T(8,128)(2,1)S(1)} %copy-done, f32[128,7168]{1,0:T(8,128)S(1)} %get-tuple-element.10, f32[128]{0:T(128)S(1)} %get-tuple-element.6, ...), kind=kLoop, calls=%fused_computation.61 | loop fusion | flops 9167872 | bytes 9233920 | tf_op jit(solution)/shard_map/reduce_sum | solution.py:134
  145.8 41.3 %psum.7 = f32[7168]{0:T(1024)} all-reduce(f32[7168]{0:T(1024)S(1)} %get-tuple-element.3), channel_id=1, replica_groups=mesh['dp'=4,'expert'=8] {'dp','expert'}, use_global_device_ids=true, to_apply=%region_10.11 | all-reduce | flops 7168 | bytes 57344 | tf_op jit(solution)/shard_map/psum | solution.py:134
  187.2 0.1 convert_reduce_fusion.1
  187.3 4.4 %fusion.2 = bf16[128,7168]{1,0:T(8,128)(2,1)} fusion(f32[4,8,7168]{2,1,0:T(8,128)S(1)} %convert_reduce_fusion.1, bf16[128,7168]{1,0:T(8,128)(2,1)S(1)} %copy-done, f32[7168]{0:T(1024)S(1)} %copy-done.3, f32[128,4]{0,1:T(4,128)S(1)} %select_reduce_fusion.1, s32[128,4]{0,1:T(4,128)S(1)} %add_select_fusion), kind=kOutput, calls=%fused_computation.6 | convolution fusion | flops 355999744 | bytes 4620288 | tf_op jit(solution)/shard_map/dot_general | solution.py:75
  (22 shorter events, 0.1 us)
Async XLA Ops:
  106.3 27.2 %all-to-all-start.2 = ((bf16[8,8,7168]{2,1,0:T(8,128)(2,1)}), bf16[8,8,7168]{2,1,0:T(8,128)(2,1)S(1)}, u32[]{:S(2)}, u32[]{:S(2)}) async-start(bf16[8,8,7168]{2,1,0:T(8,128)(2,1)} %fusion.5), calls=%async_computation.2 | async-start | bytes 1835008 | tf_op jit(solution)/shard_map/all_to_all | solution.py:113
  109.8 28.2 %copy-start.6 = (s32[128,8]{0,1:T(8,128)S(1)}, s32[128,8]{0,1:T(8,128)}, u32[]{:S(2)}) copy-start(s32[128,8]{0,1:T(8,128)} %param.13) | copy-start | bytes 12292
  109.8 28.2 %copy-start.5 = (s32[128,8]{0,1:T(8,128)S(1)}, s32[128,8]{0,1:T(8,128)}, u32[]{:S(2)}) copy-start(s32[128,8]{0,1:T(8,128)} %param.12) | copy-start | bytes 12292
  118.6 20.9 %copy-start = (bf16[128,7168]{1,0:T(8,128)(2,1)S(1)}, bf16[128,7168]{1,0:T(8,128)(2,1)}, u32[]{:S(2)}) copy-start(bf16[128,7168]{1,0:T(8,128)(2,1)} %param.9) | copy-start | bytes 5505028
  118.6 20.9 %copy-start.3 = (f32[7168]{0:T(1024)S(1)}, f32[7168]{0:T(1024)}, u32[]{:S(2)}) copy-start(f32[7168]{0:T(1024)} %param.10) | copy-start | bytes 86020
  118.6 20.9 %copy-start.4 = (f32[7168]{0:T(1024)S(1)}, f32[7168]{0:T(1024)}, u32[]{:S(2)}) copy-start(f32[7168]{0:T(1024)} %param.11) | copy-start | bytes 86020
  133.5 0.9 copy-start.2
  134.4 52.7 %all-to-all-start.1 = ((bf16[8,8,7168]{2,1,0:T(8,128)(2,1)}), bf16[8,8,7168]{2,1,0:T(8,128)(2,1)S(1)}, u32[]{:S(2)}, u32[]{:S(2)}) async-start(bf16[8,8,7168]{2,1,0:T(8,128)(2,1)} %fusion.4), calls=%async_computation.1 | async-start | bytes 1835008 | tf_op jit(solution)/shard_map/all_to_all | solution.py:105
  139.5 3.7 %copy-start.1 = (bf16[128,7168]{1,0:T(8,128)(2,1)S(1)}, bf16[128,7168]{1,0:T(8,128)(2,1)}, u32[]{:S(2)}) copy-start(bf16[128,7168]{1,0:T(8,128)(2,1)} %param.17) | copy-start | bytes 5505028
where the time goes:
time: 192 us
  blocking collectives  90.9 us (47%)
  matrix products  62.8 us (33%)
  waiting for transfers between devices  14.9 us (8%)
  other arithmetic  9.82 us (5%)
  starting transfers between devices  7.11 us (4%)
  local copies, waits for them, and re-layouts  5.27 us (3%)
    all_to_all x1, blocking collectives, shards(): lax.all_to_all(sending, 'expert', split_axis=0, concat_axis=0, tiled=True)  49.6 us
    psum x1, blocking collectives, shards(): steer_grad = lax.psum(jnp.sum(total_grad, axis=0), ('dp', 'expert'))  41.3 us
    all_to_all x1, waiting for transfers between devices, shards(): lax.all_to_all(backward.reshape(expert_count, capacity, feature_count), '...  14.9 us
    dot_general x1, matrix products, share_backward(): lax.dot_general(back_up, up_cols, contract, preferred_element_type=jnp.fl...  10.9 us
    dot_general x1, matrix products, share_backward(): lax.dot_general(back_gate, gate_cols, contract, preferred_element_type=jn...  9.73 us
    dot_general x1, matrix products, share_backward(): lax.dot_general(grad_rows, down_rows, contract, preferred_element_type=jn...  9.72 us
    dot_general x1, matrix products, share_forward(): jnp.dot(hidden, down_rows, preferred_element_type=jnp.float32)  8.77 us
    dot_general x2, matrix products, apply_combine(): return jnp.dot(combine, partial_sums, precision=lax.Precision.HIGHEST)  8 us
  transfers between devices with their start and end apart: 2, of which 1 were waited for; matrix products, arithmetic and copies ran while one was open for 9% of the time, Pallas kernels for 0%

commit v1 on v0

--- a/solution.py
+++ b/solution.py
@@ -7,6 +7,22 @@
 CAP = 8
 EPSILON = 1e-06
 GATE_UNIT = 1.0 / 65536.0
+
+
+def pairwise_exchange(x, axis, split, join):
+    ways, here = (lax.axis_size(axis), lax.axis_index(axis))
+    width = x.shape[split] // ways
+    lengths = list(x.shape)
+    lengths[split] = width
+    height = lengths[join]
+    lengths[join] = height * ways
+    full = jnp.zeros(lengths, x.dtype)
+    for mask in range(ways):
+        part = lax.dynamic_slice_in_dim(x, (here ^ mask) * width, width, axis=split)
+        if mask:
+            part = lax.ppermute(part, axis, [(d, d ^ mask) for d in range(ways)])
+        full = lax.dynamic_update_slice_in_dim(full, part, (here ^ mask) * height, axis=join)
+    return full
 
 
 def slot_tables(route_ids, route_gates, flight, capacity):
@@ -98,7 +114,7 @@
         axis=1,
     )
     sending = jnp.repeat(packed, group_size, axis=0)
-    arrived = lax.all_to_all(sending, "expert", split_axis=0, concat_axis=0, tiled=True)
+    arrived = pairwise_exchange(sending, "expert", 0, 0)
     local_rows = arrived[:, 0].reshape(expert_count * capacity, feature_count)
     local_grads = arrived[:, 1].reshape(expert_count * capacity, feature_count)
     forward, gate_pre, up_pre = share_forward(local_rows, gate_weight, up_weight, down_weight)

time: 192 us -> 185 us (0.964)
  blocking collectives: 90.9 us -> 41.1 us
  waiting for transfers between devices: 14.9 us -> 40.5 us
  starting transfers between devices: 7.11 us -> 28.1 us
  matrix products: 62.8 us -> 58 us
    all_to_all x1 -> x0, blocking collectives: 49.6 us -> none  [shards(): lax.all_to_all(sending, 'expert', split_axis=0, concat_axis=0, tiled=True)]
    ppermute x0 -> x7, waiting for transfers between devices: none -> 25.6 us  [pairwise_exchange(): part = lax.ppermute(part, axis, [(d, d ^ mask) for d in range(ways)])]
    all_to_all x1, starting transfers between devices: 3.55 us -> 14.3 us  [shards(): lax.all_to_all(backward.reshape(expert_count, capacity, feature_count), '...]
    ppermute x0 -> x7, starting transfers between devices: none -> 10 us  [pairwise_exchange(): part = lax.ppermute(part, axis, [(d, d ^ mask) for d in range(ways)])]
    dot_general x1, matrix products: 7.85 us -> 2.68 us  [share_forward(): jnp.dot(token_rows, gate_cols, preferred_element_type=jnp.float32)]
  transfers between devices with their start and end apart: 2 -> 9, of which waited for: 1 -> 6; matrix products, arithmetic and copies ran while one was open for 9% -> 9% of each run, Pallas kernels for 0% -> 0%
where the time goes in v1:
time: 185 us; the launch traced here: 184 us
  matrix products  58 us (31%)
  blocking collectives  41.1 us (22%)
  waiting for transfers between devices  40.5 us (22%)
  starting transfers between devices  28.1 us (15%)
  other arithmetic  9.82 us (5%)
  local copies, waits for them, and re-layouts  5.77 us (3%)
    psum x1, blocking collectives, shards(): steer_grad = lax.psum(jnp.sum(total_grad, axis=0), ('dp', 'expert'))  41.1 us
    ppermute x7, waiting for transfers between devices, pairwise_exchange(): part = lax.ppermute(part, axis, [(d, d ^ mask) for d in range(ways)])  25.6 us
    all_to_all x1, waiting for transfers between devices, shards(): lax.all_to_all(backward.reshape(expert_count, capacity, feature_count), '...  14.9 us
    all_to_all x1, starting transfers between devices, shards(): lax.all_to_all(backward.reshape(expert_count, capacity, feature_count), '...  14.3 us
    dot_general x1, matrix products, share_backward(): lax.dot_general(back_up, up_cols, contract, preferred_element_type=jnp.fl...  10.7 us
    ppermute x7, starting transfers between devices, pairwise_exchange(): part = lax.ppermute(part, axis, [(d, d ^ mask) for d in range(ways)])  10 us
    dot_general x1, matrix products, share_backward(): lax.dot_general(back_gate, gate_cols, contract, preferred_element_type=jn...  9.93 us
    dot_general x1, matrix products, share_backward(): lax.dot_general(grad_rows, down_rows, contract, preferred_element_type=jn...  9.88 us
  transfers between devices with their start and end apart: 9, of which 6 were waited for; matrix products, arithmetic and copies ran while one was open for 9% of the time, Pallas kernels for 0%

profile of v1, /device:TPU:0, one launch (start us, length us, event | category | flops | bytes accessed | tf_op | source)
XLA Modules:
  0.0 184.3 jit_solution(13174777172779912769)
XLA Ops:
  0.6 0.7 fusion.16
  2.2 2.1 %multiply_reduce_fusion.1 = f32[128]{0:T(128)S(1)} fusion(bf16[128,7168]{1,0:T(8,128)(2,1)} %param.9, f32[7168]{0:T(1024)} %param.10), kind=kLoop, calls=%fused_computation.15 | loop fusion | flops 3669888 | bytes 1864192 | tf_op jit(solution)/shard_map/reduce_sum | solution.py:53
  4.2 2.1 %multiply_convert_fusion = bf16[128,7168]{1,0:T(8,128)(2,1)S(1)} fusion(bf16[128,7168]{1,0:T(8,128)(2,1)} %param.9, f32[7168]{0:T(1024)} %param.11, f32[128]{0:T(128)S(1)} %get-tuple-element.14, f32[7168]{0:T(1024)} %param.10), kind=kLoop, calls=%fused_computation.14 | loop fusion | flops 4587520 | bytes 3727872 | tf_op jit(solution)/shard_map/convert_element_type | solution.py:54
  6.3 0.8 gather_fusion
  7.2 3.0 %gather_fusion.1 = bf16[32,7168]{1,0:T(8,128)(2,1)S(1)} fusion(bf16[128,7168]{1,0:T(8,128)(2,1)} %param.17, s32[1024]{0:T(1024)S(1)} %pad_clamp_fusion), kind=kCustom, calls=%fused_computation.1 | custom fusion | bytes 917632 | tf_op jit(solution)/shard_map/gather | solution.py:47
  10.5 0.2 broadcast_in_dim.88
  10.9 0.2 constant_dynamic-slice_fusion.6
  11.0 0.6 collective-permute-start
  11.6 2.6 %collective-permute-start.1 = (bf16[1,2,8,7168]{3,2,1,0:T(8,128)(2,1)S(1)}, bf16[1,2,8,7168]{3,2,1,0:T(8,128)(2,1)S(1)}, u32[]{:S(2)}, u32[]{:S(2)}) collective-permute-start(bf16[1,2,8,7168]{3,2,1,0:T(8,128)(2,1)S(1)} %get-tuple-element.10), channel_id=1, source_target_pairs={{0,2},{1,3},{2,0},{3,1},{4,6},{5,7},{6,4},{7,5},{8,10},{9,11},{10,... | collective-permute-start | bytes 688136 | tf_op jit(solution)/shard_map/ppermute | solution.py:23
  14.3 2.8 %collective-permute-start.3 = (bf16[1,2,8,7168]{3,2,1,0:T(8,128)(2,1)S(1)}, bf16[1,2,8,7168]{3,2,1,0:T(8,128)(2,1)S(1)}, u32[]{:S(2)}, u32[]{:S(2)}) collective-permute-start(bf16[1,2,8,7168]{3,2,1,0:T(8,128)(2,1)S(1)} %get-tuple-element.8), channel_id=1, source_target_pairs={{0,4},{1,5},{2,6},{3,7},{4,0},{5,1},{6,2},{7,3},{8,12},{9,13},{10,... | collective-permute-start | bytes 688136 | tf_op jit(solution)/shard_map/ppermute | solution.py:23
  17.0 3.6 %collective-permute-start.5 = (bf16[1,2,8,7168]{3,2,1,0:T(8,128)(2,1)S(1)}, bf16[1,2,8,7168]{3,2,1,0:T(8,128)(2,1)S(1)}, u32[]{:S(2)}, u32[]{:S(2)}) collective-permute-start(bf16[1,2,8,7168]{3,2,1,0:T(8,128)(2,1)S(1)} %get-tuple-element.6), channel_id=1, source_target_pairs={{0,6},{1,7},{2,4},{3,5},{4,2},{5,3},{6,0},{7,1},{8,14},{9,15},{10,... | collective-permute-start | bytes 688136 | tf_op jit(solution)/shard_map/ppermute | solution.py:23
  20.7 9.4 %collective-permute-done.1 = bf16[1,2,8,7168]{3,2,1,0:T(8,128)(2,1)S(1)} collective-permute-done((bf16[1,2,8,7168]{3,2,1,0:T(8,128)(2,1)S(1)}, bf16[1,2,8,7168]{3,2,1,0:T(8,128)(2,1)S(1)}, u32[]{:S(2)}, u32[]{:S(2)}) %collective-permute-start.1) | collective-permute-done | bytes 229408 | tf_op jit(solution)/shard_map/ppermute | solution.py:23
  30.0 0.4 collective-permute-start.6
  30.5 4.0 %collective-permute-done.2 = bf16[1,2,8,7168]{3,2,1,0:T(8,128)(2,1)S(1)} collective-permute-done((bf16[1,2,8,7168]{3,2,1,0:T(8,128)(2,1)S(1)}, bf16[1,2,8,7168]{3,2,1,0:T(8,128)(2,1)S(1)}, u32[]{:S(2)}, u32[]{:S(2)}) %collective-permute-start.2) | collective-permute-done | bytes 229408 | tf_op jit(solution)/shard_map/ppermute | solution.py:23
  34.5 0.5 collective-permute-done.4
  35.1 7.9 %collective-permute-done.5 = bf16[1,2,8,7168]{3,2,1,0:T(8,128)(2,1)S(1)} collective-permute-done((bf16[1,2,8,7168]{3,2,1,0:T(8,128)(2,1)S(1)}, bf16[1,2,8,7168]{3,2,1,0:T(8,128)(2,1)S(1)}, u32[]{:S(2)}, u32[]{:S(2)}) %collective-permute-start.5) | collective-permute-done | bytes 229408 | tf_op jit(solution)/shard_map/ppermute | solution.py:23
  43.0 3.8 %collective-permute-done.6 = bf16[1,2,8,7168]{3,2,1,0:T(8,128)(2,1)S(1)} collective-permute-done((bf16[1,2,8,7168]{3,2,1,0:T(8,128)(2,1)S(1)}, bf16[1,2,8,7168]{3,2,1,0:T(8,128)(2,1)S(1)}, u32[]{:S(2)}, u32[]{:S(2)}) %collective-permute-start.6) | collective-permute-done | bytes 229408 | tf_op jit(solution)/shard_map/ppermute | solution.py:23
  46.8 9.9 %fusion.6 = f32[64,1024]{1,0:T(8,128)S(1)} fusion(bf16[1024,7168]{1,0:T(8,128)(2,1)} %param.16, bf16[8,2,8,7168]{3,2,1,0:T(8,128)(2,1)S(1)} %constant_dynamic-update-slice_fusion.6), kind=kOutput, calls=%fused_computation.20 | convolution fusion | flops 939524096 | bytes 15859712 | tf_op jit(solution)/shard_map/dot_general | solution.py:75
  56.7 8.0 %fusion.7 = f32[64,1024]{1,0:T(8,128)S(1)} fusion(bf16[7168,1024]{1,0:T(8,128)(2,1)} %param.15, bf16[8,2,8,7168]{3,2,1,0:T(8,128)(2,1)S(1)} %constant_dynamic-update-slice_fusion.6), kind=kOutput, calls=%fused_computation.23 | convolution fusion | flops 939524096 | bytes 15859712 | tf_op jit(solution)/shard_map/dot_general | solution.py:67
  64.8 2.7 %fusion.8 = f32[64,1024]{1,0:T(8,128)S(1)} fusion(bf16[7168,1024]{1,0:T(8,128)(2,1)S(1)} %bitcast.45, bf16[8,2,8,7168]{3,2,1,0:T(8,128)(2,1)S(1)} %constant_dynamic-update-slice_fusion.6), kind=kOutput, calls=%fused_computation.24 | convolution fusion | flops 939524096 | bytes 15859712 | tf_op jit(solution)/shard_map/dot_general | solution.py:66
  67.5 9.9 %fusion.9 = f32[64,7168]{1,0:T(8,128)S(1)} fusion(bf16[7168,1024]{1,0:T(8,128)(2,1)} %param.14, f32[64,1024]{1,0:T(8,128)S(1)} %fusion.8, f32[64,1024]{1,0:T(8,128)S(1)} %fusion.6, f32[64,1024]{1,0:T(8,128)S(1)} %fusion.7), kind=kOutput, calls=%fused_computation.32 | convolution fusion | flops 940179456 | bytes 17301504 | tf_op jit(solution)/shard_map/dot_general | solution.py:83
  77.4 10.7 %fusion.5 = bf16[8,8,7168]{2,1,0:T(8,128)(2,1)} fusion(f32[64,7168]{1,0:T(8,128)S(1)} %fusion.9, bf16[7168,1024]{1,0:T(8,128)(2,1)} %param.15, f32[64,1024]{1,0:T(8,128)S(1)} %fusion.6, f32[64,1024]{1,0:T(8,128)S(1)} %fusion.8), kind=kOutput, calls=%fused_computation.11 | convolution fusion | flops 940834816 | bytes 17956864 | tf_op jit(solution)/shard_map/dot_general | solution.py:84
  88.1 14.3 %all-to-all-start.1 = ((bf16[8,8,7168]{2,1,0:T(8,128)(2,1)}), bf16[8,8,7168]{2,1,0:T(8,128)(2,1)S(1)}, u32[]{:S(2)}, u32[]{:S(2)}) async-start(bf16[8,8,7168]{2,1,0:T(8,128)(2,1)} %fusion.5), calls=%async_computation.1 | async-start | bytes 1835008 | tf_op jit(solution)/shard_map/all_to_all | solution.py:129
  102.4 8.8 %fusion.4 = bf16[8,8,7168]{2,1,0:T(8,128)(2,1)} fusion(bf16[1024,7168]{1,0:T(8,128)(2,1)} %param.16, f32[64,1024]{1,0:T(8,128)S(1)} %fusion.7, f32[64,1024]{1,0:T(8,128)S(1)} %fusion.8), kind=kOutput, calls=%fused_computation.10 | convolution fusion | flops 940376064 | bytes 16121856 | tf_op jit(solution)/shard_map/dot_general | solution.py:69
  111.2 14.9 %all-to-all-done.1 = bf16[8,8,7168]{2,1,0:T(8,128)(2,1)S(1)} async-done(((bf16[8,8,7168]{2,1,0:T(8,128)(2,1)}), bf16[8,8,7168]{2,1,0:T(8,128)(2,1)S(1)}, u32[]{:S(2)}, u32[]{:S(2)}) %all-to-all-start.1) | async-done | bytes 917536 | tf_op jit(solution)/shard_map/all_to_all | solution.py:129
  126.2 0.9 copy-done.2
  127.1 3.8 %all-to-all-start = ((bf16[8,8,7168]{2,1,0:T(8,128)(2,1)}), bf16[8,8,7168]{2,1,0:T(8,128)(2,1)S(1)}, u32[]{:S(2)}, u32[]{:S(2)}) async-start(bf16[8,8,7168]{2,1,0:T(8,128)(2,1)} %fusion.4), calls=%async_computation | async-start | bytes 1835008 | tf_op jit(solution)/shard_map/all_to_all | solution.py:121
  130.9 1.4 convert_reduce_fusion
  132.4 3.7 %multiply_reduce_fusion = (f32[128]{0:T(128)S(1)}, f32[128,7168]{1,0:T(8,128)S(1)}) fusion(bf16[128,7168]{1,0:T(8,128)(2,1)S(1)} %copy-done, f32[7168]{0:T(1024)S(1)} %copy-done.3, f32[7168]{0:T(1024)S(1)} %copy-done.4, f32[4,8,7168]{2,1,0:T(8,128)S(1)} %convert_reduce_fusion, f32[128,4]{0,1:T(4,128)S(1)} %select_reduce_fusion.1, ...), kind=kOutput, calls=%fused_computation.13 | convolution fusion | flops 356917120 | bytes 6484480 | tf_op jit(solution)/shard_map/dot_general | solution.py:91
  136.1 2.6 %fusion.28 = (f32[7168]{0:T(1024)S(1)}, bf16[128,7168]{1,0:T(8,128)(2,1)}) fusion(f32[128]{0:T(128)S(1)} %broadcast_multiply_fusion, f32[128]{0:T(128)S(1)} %get-tuple-element.13, f32[7168]{0:T(1024)S(1)} %copy-done.3, bf16[128,7168]{1,0:T(8,128)(2,1)S(1)} %copy-done, f32[128,7168]{1,0:T(8,128)S(1)} %get-tuple-element.18, f32[128]{0:T(128)S(1)} %get-tuple-element.14, ...), kind=kLoop, calls=%fused_computation.76 | loop fusion | flops 9167872 | bytes 9233920 | tf_op jit(solution)/shard_map/reduce_sum | solution.py:150
  138.7 41.1 %psum.7 = f32[7168]{0:T(1024)} all-reduce(f32[7168]{0:T(1024)S(1)} %get-tuple-element.3), channel_id=1, replica_groups=mesh['dp'=4,'expert'=8] {'dp','expert'}, use_global_device_ids=true, to_apply=%region_10.11 | all-reduce | flops 7168 | bytes 57344 | tf_op jit(solution)/shard_map/psum | solution.py:150
  179.9 4.3 %fusion.2 = bf16[128,7168]{1,0:T(8,128)(2,1)} fusion(f32[4,8,7168]{2,1,0:T(8,128)S(1)} %convert_reduce_fusion.1, bf16[128,7168]{1,0:T(8,128)(2,1)S(1)} %copy-done, f32[7168]{0:T(1024)S(1)} %copy-done.3, f32[128,4]{0,1:T(4,128)S(1)} %select_reduce_fusion.1, s32[128,4]{0,1:T(4,128)S(1)} %add_select_fusion), kind=kOutput, calls=%fused_computation.6 | convolution fusion | flops 355999744 | bytes 4620288 | tf_op jit(solution)/shard_map/dot_general | solution.py:91
  (53 shorter events, 1.6 us)
Async XLA Ops:
  11.0 6.0 %collective-permute-start = (bf16[1,2,8,7168]{3,2,1,0:T(8,128)(2,1)S(1)}, bf16[1,2,8,7168]{3,2,1,0:T(8,128)(2,1)S(1)}, u32[]{:S(2)}, u32[]{:S(2)}) collective-permute-start(bf16[1,2,8,7168]{3,2,1,0:T(8,128)(2,1)S(1)} %get-tuple-element.11), channel_id=1, source_target_pairs={{0,1},{1,0},{2,3},{3,2},{4,5},{5,4},{6,7},{7,6},{8,9},{9,8},{10,11... | collective-permute-start | bytes 688136 | tf_op jit(solution)/shard_map/ppermute | solution.py:23
  11.6 18.4 %collective-permute-start.1 = (bf16[1,2,8,7168]{3,2,1,0:T(8,128)(2,1)S(1)}, bf16[1,2,8,7168]{3,2,1,0:T(8,128)(2,1)S(1)}, u32[]{:S(2)}, u32[]{:S(2)}) collective-permute-start(bf16[1,2,8,7168]{3,2,1,0:T(8,128)(2,1)S(1)} %get-tuple-element.10), channel_id=1, source_target_pairs={{0,2},{1,3},{2,0},{3,1},{4,6},{5,7},{6,4},{7,5},{8,10},{9,11},{10,... | collective-permute-start | bytes 688136 | tf_op jit(solution)/shard_map/ppermute | solution.py:23
  14.2 20.2 %collective-permute-start.2 = (bf16[1,2,8,7168]{3,2,1,0:T(8,128)(2,1)S(1)}, bf16[1,2,8,7168]{3,2,1,0:T(8,128)(2,1)S(1)}, u32[]{:S(2)}, u32[]{:S(2)}) collective-permute-start(bf16[1,2,8,7168]{3,2,1,0:T(8,128)(2,1)S(1)} %get-tuple-element.9), channel_id=1, source_target_pairs={{0,3},{1,2},{2,1},{3,0},{4,7},{5,6},{6,5},{7,4},{8,11},{9,10},{10,... | collective-permute-start | bytes 688136 | tf_op jit(solution)/shard_map/ppermute | solution.py:23
  14.3 20.2 %collective-permute-start.3 = (bf16[1,2,8,7168]{3,2,1,0:T(8,128)(2,1)S(1)}, bf16[1,2,8,7168]{3,2,1,0:T(8,128)(2,1)S(1)}, u32[]{:S(2)}, u32[]{:S(2)}) collective-permute-start(bf16[1,2,8,7168]{3,2,1,0:T(8,128)(2,1)S(1)} %get-tuple-element.8), channel_id=1, source_target_pairs={{0,4},{1,5},{2,6},{3,7},{4,0},{5,1},{6,2},{7,3},{8,12},{9,13},{10,... | collective-permute-start | bytes 688136 | tf_op jit(solution)/shard_map/ppermute | solution.py:23
  17.0 18.0 %collective-permute-start.4 = (bf16[1,2,8,7168]{3,2,1,0:T(8,128)(2,1)S(1)}, bf16[1,2,8,7168]{3,2,1,0:T(8,128)(2,1)S(1)}, u32[]{:S(2)}, u32[]{:S(2)}) collective-permute-start(bf16[1,2,8,7168]{3,2,1,0:T(8,128)(2,1)S(1)} %get-tuple-element.7), channel_id=1, source_target_pairs={{0,5},{1,4},{2,7},{3,6},{4,1},{5,0},{6,3},{7,2},{8,13},{9,12},{10,... | collective-permute-start | bytes 688136 | tf_op jit(solution)/shard_map/ppermute | solution.py:23
  17.0 25.9 %collective-permute-start.5 = (bf16[1,2,8,7168]{3,2,1,0:T(8,128)(2,1)S(1)}, bf16[1,2,8,7168]{3,2,1,0:T(8,128)(2,1)S(1)}, u32[]{:S(2)}, u32[]{:S(2)}) collective-permute-start(bf16[1,2,8,7168]{3,2,1,0:T(8,128)(2,1)S(1)} %get-tuple-element.6), channel_id=1, source_target_pairs={{0,6},{1,7},{2,4},{3,5},{4,2},{5,3},{6,0},{7,1},{8,14},{9,15},{10,... | collective-permute-start | bytes 688136 | tf_op jit(solution)/shard_map/ppermute | solution.py:23
  30.0 16.7 %collective-permute-start.6 = (bf16[1,2,8,7168]{3,2,1,0:T(8,128)(2,1)S(1)}, bf16[1,2,8,7168]{3,2,1,0:T(8,128)(2,1)S(1)}, u32[]{:S(2)}, u32[]{:S(2)}) collective-permute-start(bf16[1,2,8,7168]{3,2,1,0:T(8,128)(2,1)S(1)} %get-tuple-element.5), channel_id=1, source_target_pairs={{0,7},{1,6},{2,5},{3,4},{4,3},{5,2},{6,1},{7,0},{8,15},{9,14},{10,... | collective-permute-start | bytes 688136 | tf_op jit(solution)/shard_map/ppermute | solution.py:23
  46.8 17.9 %slice-start = ((s8[14680064]{0:T(1024)(128)(4,1)}), s8[4194304]{0:T(1024)(128)(4,1)S(1)}, s32[]{:S(2)}) async-start(s8[14680064]{0:T(1024)(128)(4,1)} %bitcast.44), calls=%async_computation.2 | async-start | bytes 8388608
  46.8 17.9 %slice-start.1 = ((s8[14680064]{0:T(1024)(128)(4,1)}), s8[2097152]{0:T(1024)(128)(4,1)S(1)}, s32[]{:S(2)}) async-start(s8[14680064]{0:T(1024)(128)(4,1)} %bitcast.44), calls=%async_computation.3 | async-start | bytes 4194304
  56.7 8.1 %slice-start.2 = ((s8[14680064]{0:T(1024)(128)(4,1)}), s8[4194304]{0:T(1024)(128)(4,1)S(1)}, s32[]{:S(2)}) async-start(s8[14680064]{0:T(1024)(128)(4,1)} %bitcast.44), calls=%async_computation.4 | async-start | bytes 8388608
  56.7 8.1 %slice-start.3 = ((s8[14680064]{0:T(1024)(128)(4,1)}), s8[4194304]{0:T(1024)(128)(4,1)S(1)}, s32[]{:S(2)}) async-start(s8[14680064]{0:T(1024)(128)(4,1)} %bitcast.44), calls=%async_computation.5 | async-start | bytes 8388608
  88.1 38.1 %all-to-all-start.1 = ((bf16[8,8,7168]{2,1,0:T(8,128)(2,1)}), bf16[8,8,7168]{2,1,0:T(8,128)(2,1)S(1)}, u32[]{:S(2)}, u32[]{:S(2)}) async-start(bf16[8,8,7168]{2,1,0:T(8,128)(2,1)} %fusion.5), calls=%async_computation.1 | async-start | bytes 1835008 | tf_op jit(solution)/shard_map/all_to_all | solution.py:129
  102.4 28.5 %copy-start.6 = (s32[128,8]{0,1:T(8,128)S(1)}, s32[128,8]{0,1:T(8,128)}, u32[]{:S(2)}) copy-start(s32[128,8]{0,1:T(8,128)} %param.13) | copy-start | bytes 12292
  102.4 28.5 %copy-start.5 = (s32[128,8]{0,1:T(8,128)S(1)}, s32[128,8]{0,1:T(8,128)}, u32[]{:S(2)}) copy-start(s32[128,8]{0,1:T(8,128)} %param.12) | copy-start | bytes 12292
  111.2 21.2 %copy-start = (bf16[128,7168]{1,0:T(8,128)(2,1)S(1)}, bf16[128,7168]{1,0:T(8,128)(2,1)}, u32[]{:S(2)}) copy-start(bf16[128,7168]{1,0:T(8,128)(2,1)} %param.9) | copy-start | bytes 5505028
  111.2 21.2 %copy-start.3 = (f32[7168]{0:T(1024)S(1)}, f32[7168]{0:T(1024)}, u32[]{:S(2)}) copy-start(f32[7168]{0:T(1024)} %param.10) | copy-start | bytes 86020
  111.2 21.2 %copy-start.4 = (f32[7168]{0:T(1024)S(1)}, f32[7168]{0:T(1024)}, u32[]{:S(2)}) copy-start(f32[7168]{0:T(1024)} %param.11) | copy-start | bytes 86020
  126.2 0.9 copy-start.2
  127.1 52.7 %all-to-all-start = ((bf16[8,8,7168]{2,1,0:T(8,128)(2,1)}), bf16[8,8,7168]{2,1,0:T(8,128)(2,1)S(1)}, u32[]{:S(2)}, u32[]{:S(2)}) async-start(bf16[8,8,7168]{2,1,0:T(8,128)(2,1)} %fusion.4), calls=%async_computation | async-start | bytes 1835008 | tf_op jit(solution)/shard_map/all_to_all | solution.py:121
  132.4 3.7 %copy-start.1 = (bf16[128,7168]{1,0:T(8,128)(2,1)S(1)}, bf16[128,7168]{1,0:T(8,128)(2,1)}, u32[]{:S(2)}) copy-start(bf16[128,7168]{1,0:T(8,128)(2,1)} %param.17) | copy-start | bytes 5505028
